TPU v7x, 32 devices: a whole 2x2x4 slice. The times are simulated.
32 devices in a mesh: rep: 8 (over z, x), shard: 4 (over y, core).
Axes of the slice: x: 2, y: 2, z: 4, core: 2. Of those that a mesh axis runs over, the one named last changes fastest.
Arguments:
- tokens: bfloat16 [32, 384, 1024], P(('rep', 'shard')), may hold values from -6 to 6
- cont_segment: int32 [32, 2, 64], P(('rep', 'shard')), may hold values from 0 to 1, as said below
- cotangent: bfloat16 [32, 384, 1024], P(('rep', 'shard')), may hold values from -6 to 6
- ln1_gain: bfloat16 [1024], P('shard'), may hold values from 0.099609375 to 1.8984375
- ln1_bias: bfloat16 [1024], P('shard'), may hold values from -3 to 3
- w_qkv: bfloat16 [1024, 3072], P(None, 'shard'), may hold values from -0.1875 to 0.1875
- q_bias: bfloat16 [1024], P('shard'), may hold values from -3 to 3
- v_bias: bfloat16 [1024], P('shard'), may hold values from -3 to 3
- w_out: bfloat16 [1024, 1024], P('shard'), may hold values from -0.75 to 0.75
- b_out: bfloat16 [1024], P('shard'), may hold values from -3 to 3
- ln2_gain: bfloat16 [1024], P('shard'), may hold values from 0.099609375 to 1.8984375
- ln2_bias: bfloat16 [1024], P('shard'), may hold values from -3 to 3
- w_up: bfloat16 [1024, 4096], P(None, 'shard'), may hold values from -0.1875 to 0.1875
- b_up: bfloat16 [4096], P('shard'), may hold values from -3 to 3
- w_down: bfloat16 [4096, 1024], P('shard'), may hold values from -0.125 to 0.125
- b_down: bfloat16 [1024], P('shard'), may hold values from -3 to 3
Outputs:
- layer_out: bfloat16 [32, 384, 1024], P(('rep', 'shard'))
- grad_tokens: bfloat16 [32, 384, 1024], P(('rep', 'shard'))
- grad_ln1_gain: float32 [1024], P('shard')
- grad_ln1_bias: float32 [1024], P('shard')
- grad_w_qkv: float32 [1024, 3072], P(None, 'shard')
- grad_q_bias: float32 [1024], P('shard')
- grad_v_bias: float32 [1024], P('shard')
- grad_w_out: float32 [1024, 1024], P('shard')
- grad_b_out: float32 [1024], P('shard')
- grad_ln2_gain: float32 [1024], P('shard')
- grad_ln2_bias: float32 [1024], P('shard')
- grad_w_up: float32 [1024, 4096], P(None, 'shard')
- grad_b_up: float32 [4096], P('shard')
- grad_w_down: float32 [4096, 1024], P('shard')
- grad_b_down: float32 [1024], P('shard')
Inputs may be any that keep to these rules, and one draw needn't show every extreme that they name: `cont_segment`: each micro-batch holds 2 continuations, numbers never falling, each of 16 to 48 rows; in the first micro-batch of every prompt one continuation has exactly 48 rows.
All inputs are finite; a program needn't handle non-finite values.
Results may differ from a plain program's by a relative error of at most 0.015.
Values may be sent and summed in bfloat16 or wider, within the bound.
No kernel may reach another device: no remote copies, remote signals or barrier semaphores. Data moves between devices by JAX's collectives and lax.ppermute only.
A program may use at most 256 MiB of HBM per device.

v0:
```python
from functools import partial
import jax
import jax.numpy as jnp
from jax import lax
from jax.sharding import PartitionSpec as P

HEADS = 16
HDIM = 64
PROMPT = 256


def normalize(values, gain, shift):
    center = values - jnp.mean(values, -1, keepdims=True)
    spread = jnp.mean(center * center, -1, keepdims=True)
    return center * lax.rsqrt(spread + 1e-05) * gain + shift


def layout(segments):
    micros, row_count = segments.shape
    same_seg = segments[:, :, None] == segments[:, None, :]
    earlier = jnp.arange(row_count)[None, :] < jnp.arange(row_count)[:, None]
    offsets = jnp.sum(jnp.where(same_seg & earlier[None], 1, 0), -1).astype(jnp.int32)
    cont_pos = PROMPT + offsets
    owners = jnp.arange(micros, dtype=jnp.int32)[:, None] * row_count + segments
    positions = jnp.concatenate([jnp.arange(PROMPT, dtype=jnp.int32), cont_pos.reshape(-1)])
    groups = jnp.concatenate([jnp.full((PROMPT,), -1, jnp.int32), owners.reshape(-1)])
    places = jnp.arange(positions.shape[0], dtype=jnp.int32)
    allowed = (places[None, :] <= places[:, None]) & (
        (places[None, :] < PROMPT) | (groups[None, :] == groups[:, None])
    )
    distance = (positions[:, None] - positions[None, :]).astype(jnp.float32)
    return (distance, allowed)


def head_slice(matrix, block):
    block_width = 4 * HDIM
    part = lax.dynamic_slice_in_dim(matrix, block * block_width, block_width, 1)
    return part.reshape(matrix.shape[0], 4, HDIM)


def block_scores(q_part, k_part, block, distance, allowed):
    heads = (block * 4 + jnp.arange(4, dtype=jnp.int32)).astype(jnp.float32)
    slopes = jnp.exp2(-8.0 * (heads + 1.0) / HEADS)
    scores = jnp.einsum(
        "qhd,khd->hqk", q_part, k_part, preferred_element_type=jnp.float32
    ) * HDIM ** (-0.5)
    scores = scores - slopes[:, None, None] * distance[None]
    return jnp.where(allowed[None], scores, -jnp.inf)


def side_by_side(blocks):
    return jnp.transpose(blocks, (1, 0, 2)).reshape(
        blocks.shape[1], blocks.shape[0] * blocks.shape[2]
    )


def attend_forward(queries, key_rows, values, distance, allowed):
    length = queries.shape[0]

    def head_block(block):
        q_part = head_slice(queries, block)
        k_part = head_slice(key_rows, block)
        v_part = head_slice(values, block)
        scores = block_scores(q_part, k_part, block, distance, allowed)
        peak = jnp.max(scores, -1, keepdims=True)
        exps_rel = jnp.exp(scores - peak)
        row_totals = jnp.sum(exps_rel, -1, keepdims=True)
        attn_probs = (exps_rel / row_totals).astype(jnp.bfloat16)
        mixed = jnp.einsum("hqk,khd->qhd", attn_probs, v_part, preferred_element_type=jnp.float32)
        return (mixed.reshape(length, 4 * HDIM), (peak + jnp.log(row_totals))[:, :, 0])

    mixed, log_norms = lax.map(head_block, jnp.arange(HEADS // 4, dtype=jnp.int32))
    return (side_by_side(mixed).astype(jnp.bfloat16), log_norms)


def attend_backward(queries, key_rows, values, grad_mixed, log_norms, distance, allowed):
    length = queries.shape[0]
    scale = HDIM ** (-0.5)

    def head_block(block):
        q_part = head_slice(queries, block)
        k_part = head_slice(key_rows, block)
        v_part = head_slice(values, block)
        g_part = head_slice(grad_mixed, block)
        scores = block_scores(q_part, k_part, block, distance, allowed)
        attn_probs = jnp.exp(scores - log_norms[block][:, :, None])
        grad_probs = jnp.einsum("qhd,khd->hqk", g_part, v_part, preferred_element_type=jnp.float32)
        inner = jnp.sum(attn_probs * grad_probs, -1, keepdims=True)
        grad_scores = (attn_probs * (grad_probs - inner)).astype(jnp.bfloat16)
        grad_q = (
            jnp.einsum("hqk,khd->qhd", grad_scores, k_part, preferred_element_type=jnp.float32)
            * scale
        )
        grad_k = (
            jnp.einsum("hqk,qhd->khd", grad_scores, q_part, preferred_element_type=jnp.float32)
            * scale
        )
        grad_v = jnp.einsum(
            "hqk,qhd->khd",
            attn_probs.astype(jnp.bfloat16),
            g_part,
            preferred_element_type=jnp.float32,
        )
        block_width = 4 * HDIM
        return (
            grad_q.reshape(length, block_width),
            grad_k.reshape(length, block_width),
            grad_v.reshape(length, block_width),
        )

    grad_q, grad_k, grad_v = lax.map(head_block, jnp.arange(HEADS // 4, dtype=jnp.int32))
    return (
        side_by_side(grad_q).astype(jnp.bfloat16),
        side_by_side(grad_k).astype(jnp.bfloat16),
        side_by_side(grad_v).astype(jnp.bfloat16),
    )


SMALL = (
    "ln1_gain",
    "ln1_bias",
    "q_bias",
    "v_bias",
    "b_out",
    "ln2_gain",
    "ln2_bias",
    "b_up",
    "b_down",
)


def gather_small(pieces):
    packed = jnp.concatenate(pieces)
    shards = lax.all_gather(packed, "shard", axis=0, tiled=False)
    fulls, offset = ([], 0)
    for piece in pieces:
        width = piece.shape[0]
        fulls.append(shards[:, offset : offset + width].reshape(-1))
        offset += width
    return fulls


def body(
    tokens,
    cont_segment,
    cotangent,
    ln1_gain,
    ln1_bias,
    w_qkv,
    q_bias,
    v_bias,
    w_out,
    b_out,
    ln2_gain,
    ln2_bias,
    w_up,
    b_up,
    w_down,
    b_down,
):
    shard_count = lax.psum(1, "shard")
    full_g1, full_s1, full_qb, full_vb, full_bo, full_g2, full_s2, full_bu, full_bd = gather_small(
        [ln1_gain, ln1_bias, q_bias, v_bias, b_out, ln2_gain, ln2_bias, b_up, b_down]
    )
    full_qkv = lax.all_gather(w_qkv, "shard", axis=1, tiled=True)
    full_out = lax.all_gather(w_out, "shard", axis=0, tiled=True)
    full_up = lax.all_gather(w_up, "shard", axis=1, tiled=True)
    full_down = lax.all_gather(w_down, "shard", axis=0, tiled=True)
    inputs = tokens[0].astype(jnp.float32)
    length, model_width = inputs.shape
    distance, allowed = layout(cont_segment[0])
    normed = normalize(inputs, full_g1.astype(jnp.float32), full_s1.astype(jnp.float32)).astype(
        jnp.bfloat16
    )
    projected = jnp.dot(normed, full_qkv, preferred_element_type=jnp.float32)
    queries = (projected[:, :model_width] + full_qb.astype(jnp.float32)).astype(jnp.bfloat16)
    key_rows = projected[:, model_width : 2 * model_width].astype(jnp.bfloat16)
    values = (projected[:, 2 * model_width :] + full_vb.astype(jnp.float32)).astype(jnp.bfloat16)
    mixed, log_norms = attend_forward(queries, key_rows, values, distance, allowed)
    branch = jnp.dot(mixed, full_out, preferred_element_type=jnp.float32) + full_bo.astype(
        jnp.float32
    )
    middle = inputs + branch
    normed_two = normalize(middle, full_g2.astype(jnp.float32), full_s2.astype(jnp.float32)).astype(
        jnp.bfloat16
    )
    pre_act = jnp.dot(normed_two, full_up, preferred_element_type=jnp.float32) + full_bu.astype(
        jnp.float32
    )
    activated = jax.nn.gelu(pre_act, approximate=True).astype(jnp.bfloat16)
    outputs = middle + (
        jnp.dot(activated, full_down, preferred_element_type=jnp.float32)
        + full_bd.astype(jnp.float32)
    )
    back_g1, back_qkv, back_out, back_g2, back_up, back_down = (
        full_g1,
        full_qkv,
        full_out,
        full_g2,
        full_up,
        full_down,
    )
    cot_low = cotangent[0]
    cot_full = cot_low.astype(jnp.float32)
    zero_shift = jnp.zeros((model_width,), jnp.float32)
    grad_bd = jnp.sum(cot_full, 0)
    grad_act = jnp.einsum("to,fo->tf", cot_low, back_down, preferred_element_type=jnp.float32)
    gelu_value, gelu_pull = jax.vjp(partial(jax.nn.gelu, approximate=True), pre_act)
    grad_pre = gelu_pull(grad_act)[0].astype(jnp.bfloat16)
    grad_bu = jnp.sum(grad_pre.astype(jnp.float32), 0)
    grad_normed_two = jnp.einsum("tf,if->ti", grad_pre, back_up, preferred_element_type=jnp.float32)
    norm_value_two, norm_pull_two = jax.vjp(
        normalize, middle, back_g2.astype(jnp.float32), zero_shift
    )
    grad_mid_part, grad_g2, grad_s2 = norm_pull_two(grad_normed_two)
    grad_middle = cot_full + grad_mid_part
    grad_branch = grad_middle.astype(jnp.bfloat16)
    grad_bo = jnp.sum(grad_branch.astype(jnp.float32), 0)
    grad_mixed = jnp.einsum(
        "to,io->ti", grad_branch, back_out, preferred_element_type=jnp.float32
    ).astype(jnp.bfloat16)
    grad_q, grad_k, grad_v = attend_backward(
        queries, key_rows, values, grad_mixed, log_norms, distance, allowed
    )
    grad_proj = jnp.concatenate([grad_q, grad_k, grad_v], 1)
    grad_qb = jnp.sum(grad_q.astype(jnp.float32), 0)
    grad_vb = jnp.sum(grad_v.astype(jnp.float32), 0)
    grad_normed = jnp.einsum("tc,ic->ti", grad_proj, back_qkv, preferred_element_type=jnp.float32)
    norm_value_one, norm_pull_one = jax.vjp(
        normalize, inputs, back_g1.astype(jnp.float32), zero_shift
    )
    grad_in_part, grad_g1, grad_s1 = norm_pull_one(grad_normed)
    grad_inputs = grad_middle + grad_in_part
    grad_down = jnp.einsum("tf,to->fo", activated, cot_low, preferred_element_type=jnp.float32)
    grad_up = jnp.einsum("ti,tf->if", normed_two, grad_pre, preferred_element_type=jnp.float32)
    grad_out = jnp.einsum("ti,to->io", mixed, grad_branch, preferred_element_type=jnp.float32)
    grad_qkv = jnp.einsum("ti,tc->ic", normed, grad_proj, preferred_element_type=jnp.float32)
    smalls = [grad_g1, grad_s1, grad_qb, grad_vb, grad_bo, grad_g2, grad_s2, grad_bu, grad_bd]
    small_rows = jnp.concatenate([g.reshape(shard_count, -1) for g in smalls], 1)
    small_rows = small_rows.reshape(shard_count, -1, model_width)
    small_rows = jnp.pad(small_rows, ((0, 0), (0, 16 - small_rows.shape[1]), (0, 0)))
    down_rows = grad_down.reshape(shard_count, -1, model_width)
    down_width = down_rows.shape[1] * model_width
    joined = jnp.concatenate([down_rows, small_rows], 1).reshape(-1, model_width)
    joined_own = lax.psum_scatter(
        joined.astype(jnp.bfloat16), "shard", scatter_dimension=0, tiled=True
    ).reshape(-1)
    qkv_own = lax.psum_scatter(
        grad_qkv.astype(jnp.bfloat16), "shard", scatter_dimension=1, tiled=True
    )
    out_own = lax.psum_scatter(
        grad_out.astype(jnp.bfloat16), "shard", scatter_dimension=0, tiled=True
    )
    up_own = lax.psum_scatter(
        grad_up.astype(jnp.bfloat16), "shard", scatter_dimension=1, tiled=True
    )
    owned = [qkv_own, out_own, up_own, joined_own]
    flat = jnp.concatenate([o.reshape(-1).astype(jnp.float32) for o in owned])
    total = lax.psum(flat, "rep")
    pieces, offset = ([], 0)
    for o in owned:
        pieces.append(total[offset : offset + o.size].reshape(o.shape))
        offset += o.size
    qkv_fin, out_fin, up_fin, joined_fin = pieces
    down_fin = joined_fin[:down_width].reshape(grad_down.shape[0] // shard_count, -1)
    small_fin, offset = ([], down_width)
    for g in smalls:
        width = g.shape[0] // shard_count
        small_fin.append(joined_fin[offset : offset + width])
        offset += width
    g1_fin, s1_fin, qb_fin, vb_fin, bo_fin, g2_fin, s2_fin, bu_fin, bd_fin = small_fin
    return (
        outputs.astype(jnp.bfloat16)[None],
        grad_inputs.astype(jnp.bfloat16)[None],
        g1_fin,
        s1_fin,
        qkv_fin,
        qb_fin,
        vb_fin,
        out_fin,
        bo_fin,
        g2_fin,
        s2_fin,
        up_fin,
        bu_fin,
        down_fin,
        bd_fin,
    )


def solution(mesh):
    return jax.shard_map(
        body,
        mesh=mesh,
        in_specs=(
            P(("rep", "shard"), None, None),
            P(("rep", "shard"), None, None),
            P(("rep", "shard"), None, None),
            P("shard"),
            P("shard"),
            P(None, "shard"),
            P("shard"),
            P("shard"),
            P("shard", None),
            P("shard"),
            P("shard"),
            P("shard"),
            P(None, "shard"),
            P("shard"),
            P("shard", None),
            P("shard"),
        ),
        out_specs=(
            P(("rep", "shard"), None, None),
            P(("rep", "shard"), None, None),
            P("shard"),
            P("shard"),
            P(None, "shard"),
            P("shard"),
            P("shard"),
            P("shard", None),
            P("shard"),
            P("shard"),
            P("shard"),
            P(None, "shard"),
            P("shard"),
            P("shard", None),
            P("shard"),
        ),
        check_vma=False,
    )
```

profile of v0, /device:TPU:0, one launch (start us, length us, event | category | flops | bytes accessed | tf_op | source)
XLA Modules:
  0.0 967.9 jit_solution(11583978581339955561)
XLA Ops:
  12.2 6.3 all-gather
  20.3 38.4 %all-gather.6.cloned.1.call-done = bf16[1024,3072]{1,0:T(8,128)(2,1)} async-done(((bf16[1024,768]{1,0:T(8,128)(2,1)}), bf16[1024,3072]{1,0:T(8,128)(2,1)}) %all-gather.6.cloned.1.call-update) | async-done | bytes 6291472 | tf_op jit(solution)/shard_map/all_gather | solution.py:165
  58.7 5.1 fusion.69
  65.9 1.5 copy.75
  68.4 19.0 %while.32 = (s32[]{:T(128)}, bf16[4,384,256]{1,2,0:T(8,128)(2,1)}, f32[4,4,384]{2,1,0:T(4,128)S(1)}, s32[4]{0:T(128)S(1)}, bf16[384,1024]{0,1:T(8,128)(2,1)S(1)}...) while((s32[]{:T(128)}, bf16[4,384,256]{1,2,0:T(8,128)(2,1)}, ...), condition=%wide.region_6.7_spmd.clone, body=%wide.region_3.6_spmd.clone.sunk | while | flops 157776416 | bytes 10964623 | solution.py:72
  88.6 3.0 fusion.79
  91.9 50.8 %all-gather.10.cloned.1.call-done = bf16[1024,4096]{1,0:T(8,128)(2,1)} async-done(((bf16[1024,1024]{1,0:T(8,128)(2,1)}), bf16[1024,4096]{1,0:T(8,128)(2,1)}) %all-gather.10.cloned.1.call-update) | async-done | bytes 8388624 | tf_op jit(solution)/shard_map/all_gather | solution.py:167
  142.7 11.3 %fusion.30 = (bf16[4096,384]{0,1:T(8,128)(2,1)}, f32[384,4096]{1,0:T(8,128)}) fusion(f32[4096]{0:T(1024)S(1)} %bitcast.254, bf16[1024,4096]{1,0:T(8,128)(2,1)} %all-gather.10.cloned.1.call-done, f32[384,1024]{1,0:T(8,128)S(1)} %get-tuple-element.523, f32[1024]{0:T(1024)S(1)} %bitcast.261, f32[1024]{0:T(1024)S(1)} %bitcast.255, f32[384]{0:T(512)S(1)} %fusion.61, ...), kind=kOutput, calls=%fused_computation.60 | convolution fusion | flops 3238920192 | bytes 19426304 | tf_op jit(solution)/shard_map/dot_general | solution.py:187
  154.0 48.4 %all-gather.12.cloned.1.call-done = bf16[4096,1024]{1,0:T(8,128)(2,1)} async-done(((bf16[1024,1024]{1,0:T(8,128)(2,1)}), bf16[4096,1024]{1,0:T(8,128)(2,1)}) %all-gather.12.cloned.1.call-update) | async-done | bytes 8388624 | tf_op jit(solution)/shard_map/all_gather | solution.py:168
  202.4 10.6 %fusion.80 = (bf16[4096]{0:T(1024)(128)(2,1)S(1)}, bf16[384,4096]{1,0:T(8,128)(2,1)S(1)}) fusion(f32[384,4096]{1,0:T(8,128)} %get-tuple-element.529, bf16[4096,1024]{1,0:T(8,128)(2,1)} %all-gather.12.cloned.1.call-done, bf16[1,384,1024]{2,1,0:T(8,128)(2,1)S(1)} %copy-done.10), kind=kOutput, calls=%fused_computation.158 | convolution fusion | flops 3254251520 | bytes 18620416 | tf_op jit(solution)/shard_map/to,fo->tf/dot_general | solution.py:207
  213.0 3.8 multiply_reduce_fusion.1
  217.5 1.1 copy-done.4
  219.2 2.6 convolution_convert_fusion.3
  221.8 2.6 convolution_convert_fusion.4
  227.3 45.8 %while.33 = (s32[]{:T(128)}, bf16[4,384,256]{1,2,0:T(8,128)(2,1)}, bf16[4,384,256]{1,2,0:T(8,128)(2,1)}, bf16[4,384,256]{1,2,0:T(8,128)(2,1)}, s32[4]{0:T(128)S(...) while((s32[]{:T(128)}, bf16[4,384,256]{1,2,0:T(8,128)(2,1)}, ...), condition=%wide.region_13.14_spmd.clone, body=%wide.region_11.13_spmd.clone.sunk | while | flops 385251872 | bytes 36898628 | solution.py:111
  234.5 1.1 multiply_reduce_fusion.5
  245.9 1.1 multiply_reduce_fusion.5
  257.3 1.1 multiply_reduce_fusion.5
  268.7 1.1 multiply_reduce_fusion.5
  273.1 8.2 convolution_convert_fusion.2
  281.3 1.3 copy-done.3
  282.7 9.6 convolution_convert_fusion
  293.8 6.5 fusion.72
  300.3 1.1 copy-done.13
  302.2 1.5 reduce.5
  303.8 1.4 reduce.6
  305.3 4.6 copy.86
  309.9 6.6 convolution_convert_fusion.1
  316.6 3.7 fusion.15
  320.4 1.9 copy.97
  322.3 17.0 %reduce-scatter.5.cloned.1.call-done = bf16[1024,768]{1,0:T(8,128)(2,1)} async-done(((bf16[1024,3072]{1,0:T(8,128)(2,1)}), bf16[1024,768]{1,0:T(8,128)(2,1)}) %reduce-scatter.5.cloned.1.call-update) | async-done | bytes 1572880 | tf_op jit(solution)/shard_map/reduce_scatter | solution.py:248
  339.3 4.0 convert_element_type.308
  343.3 69.8 %reduce-scatter.9.cloned.1.call-done = bf16[1024,1024]{1,0:T(8,128)(2,1)} async-done(((bf16[1024,4096]{1,0:T(8,128)(2,1)}), bf16[1024,1024]{1,0:T(8,128)(2,1)}) %reduce-scatter.9.cloned.1.call-update) | async-done | bytes 2097168 | tf_op jit(solution)/shard_map/reduce_scatter | solution.py:254
  413.2 3.5 copy.98
  416.7 71.3 %reduce-scatter.11.cloned.1.call-done = bf16[1040,1024]{1,0:T(8,128)(2,1)} async-done(((bf16[4160,1024]{1,0:T(8,128)(2,1)}), bf16[1040,1024]{1,0:T(8,128)(2,1)}) %reduce-scatter.11.cloned.1.call-update) | async-done | bytes 2129936 | tf_op jit(solution)/shard_map/reduce_scatter | solution.py:245
  488.1 2.4 copy.99
  490.8 48.4 %maximum_convert_fusion = f32[3162112]{0:T(1024)} fusion(bf16[1064960]{0:T(1024)(128)(2,1)S(1)} %bitcast.226, bf16[1048576]{0:T(1024)(128)(2,1)S(1)} %bitcast.227, bf16[262144]{0:T(1024)(128)(2,1)S(1)} %bitcast.240, bf16[786432]{0:T(1024)(128)(2,1)S(1)} %copy-done.12), kind=kLoop, calls=%fused_computation.45 | loop fusion | flops 25296896 | bytes 18972672 | tf_op jit(solution)/shard_map/concatenate | solution.py:258
  539.9 3.5 fusion.54
  543.4 11.1 %fusion.51 = bf16[1,384,1024]{2,1,0:T(8,128)(2,1)} fusion(f32[384,1024]{1,0:T(8,128)S(1)} %copy-done.3, bf16[4096,1024]{1,0:T(8,128)(2,1)} %all-gather.12.cloned.1.call-done, f32[384,4096]{1,0:T(8,128)} %get-tuple-element.529, f32[1024]{0:T(1024)S(1)} %bitcast.263), kind=kOutput, calls=%fused_computation.101 | convolution fusion | flops 3236560896 | bytes 17043456 | tf_op jit(solution)/shard_map/dot_general | solution.py:192
  554.4 380.6 %all-reduce.4.cloned.1.call-done = f32[3162112]{0:T(1024)} async-done(((f32[3162112]{0:T(1024)}), f32[3162112]{0:T(1024)}) %all-reduce.4.cloned.1.call-update) | async-done | bytes 12648464 | tf_op jit(solution)/shard_map/psum | solution.py:259
  935.0 1.9 slice-done
  936.9 2.0 reshape.407
  938.9 1.2 slice-done.1
  941.2 7.4 fusion.78
  948.6 4.9 slice.140
  953.5 4.9 slice.143
  958.4 1.4 fusion.77
  959.8 1.3 slice.167
  (296 shorter events, 61.0 us)
Async XLA Ops:
  7.2 51.5 %all-gather.6.cloned.1.call-start = ((), (), s32[]{:S(2)}) async-start(), calls=%async_computation.4 | async-start | bytes 7864320 | tf_op jit(solution)/shard_map/all_gather | solution.py:165
  7.9 2.3 copy-start.21
  7.9 2.5 copy-start.22
  7.9 2.7 copy-start.23
  7.9 2.9 copy-start.24
  8.0 3.1 copy-start.25
  8.0 3.4 copy-start.26
  8.0 3.6 copy-start.27
  8.0 3.8 copy-start.20
  8.0 4.0 copy-start.28
  8.0 79.4 %all-gather.8.cloned.1.call-start = ((), (), s32[]{:S(2)}) async-start(), calls=%async_computation.5 | async-start | bytes 2621440 | tf_op jit(solution)/shard_map/all_gather | solution.py:166
  8.8 10.5 %copy-start.19 = (s32[1,2,64]{2,1,0:T(2,128)S(1)}, s32[1,2,64]{2,1,0:T(2,128)}, u32[]{:S(2)}) copy-start(s32[1,2,64]{2,1,0:T(2,128)} %param.21) | copy-start | bytes 1540
  8.8 10.9 %copy-start = (bf16[1,384,1024]{2,1,0:T(8,128)(2,1)S(1)}, bf16[1,384,1024]{2,1,0:T(8,128)(2,1)}, u32[]{:S(2)}) copy-start(bf16[1,384,1024]{2,1,0:T(8,128)(2,1)} %param.20) | copy-start | bytes 2359300
  8.8 133.9 %all-gather.10.cloned.1.call-start = ((), (), s32[]{:S(2)}) async-start(), calls=%async_computation.6 | async-start | bytes 10485760 | tf_op jit(solution)/shard_map/all_gather | solution.py:167
  9.5 192.9 %all-gather.12.cloned.1.call-start = ((), (), s32[]{:S(2)}) async-start(), calls=%async_computation.7 | async-start | bytes 10485760 | tf_op jit(solution)/shard_map/all_gather | solution.py:168
  10.1 310.3 %reduce-scatter.7.cloned.1.call-start = ((), (), s32[]{:S(2)}) async-start(), calls=%async_computation.9 | async-start | bytes 2621440 | tf_op jit(solution)/shard_map/reduce_scatter | solution.py:251
  91.6 125.3 %copy-start.2 = (f32[384,1024]{1,0:T(8,128)}, f32[384,1024]{1,0:T(8,128)S(1)}, u32[]{:S(2)}) copy-start(f32[384,1024]{1,0:T(8,128)S(1)} %get-tuple-element.523) | copy-start | bytes 4718596
  142.7 59.7 %copy-start.10 = (bf16[1,384,1024]{2,1,0:T(8,128)(2,1)S(1)}, bf16[1,384,1024]{2,1,0:T(8,128)(2,1)}, u32[]{:S(2)}) copy-start(bf16[1,384,1024]{2,1,0:T(8,128)(2,1)} %param.22) | copy-start | bytes 2359300
  202.4 10.6 %copy-start.29 = (bf16[1024,4096]{1,0:T(8,128)(2,1)S(1)}, bf16[1024,4096]{1,0:T(8,128)(2,1)}, u32[]{:S(2)}) copy-start(bf16[1024,4096]{1,0:T(8,128)(2,1)} %all-gather.10.cloned.1.call-done) | copy-start | bytes 25165828
  213.0 3.8 copy-start.30
  217.5 1.7 copy-start.14
  221.7 117.6 %reduce-scatter.5.cloned.1.call-start = ((), (), s32[]{:S(2)}) async-start(), calls=%async_computation.8 | async-start | bytes 7864320 | tf_op jit(solution)/shard_map/reduce_scatter | solution.py:248
  227.5 2.6 copy-start.5
  227.5 2.6 copy-start.16
  237.1 1.9 copy-start.6
  237.1 1.9 copy-start.17
  239.0 2.5 copy-start.5
  239.0 2.6 copy-start.16
  248.5 1.9 copy-start.6
  248.5 1.9 copy-start.17
  250.3 2.5 copy-start.5
  250.3 2.6 copy-start.16
  259.8 1.9 copy-start.6
  259.8 1.9 copy-start.17
  261.7 2.5 copy-start.5
  261.7 2.6 copy-start.16
  271.2 1.9 copy-start.6
  271.2 1.9 copy-start.17
  281.3 1.4 copy-start.3
  281.3 131.9 %reduce-scatter.9.cloned.1.call-start = ((), (), s32[]{:S(2)}) async-start(), calls=%async_computation.10 | async-start | bytes 10485760 | tf_op jit(solution)/shard_map/reduce_scatter | solution.py:254
  292.3 1.5 copy-start.1
  292.4 195.7 %reduce-scatter.11.cloned.1.call-start = ((), (), s32[]{:S(2)}) async-start(), calls=%async_computation.11 | async-start | bytes 10649600 | tf_op jit(solution)/shard_map/reduce_scatter | solution.py:245
  320.3 614.7 %all-reduce.4.cloned.1.call-start = ((), (), s32[]{:S(2)}) async-start(), calls=%async_computation.12 | async-start | bytes 25296896 | tf_op jit(solution)/shard_map/psum | solution.py:259
  488.0 2.4 copy-start.9
  488.0 2.7 copy-start.12
  488.0 2.8 copy-start.15
  935.0 1.9 slice-start
  938.9 1.2 slice-start.1
  (6 other events, 6.3 us)
Sparse Core Ops, SparseCore 0:
  9.6 49.0 all-gather.5
  60.2 22.5 all-gather.7
  84.4 58.2 all-gather.9
  144.1 58.2 all-gather.11
  221.9 31.1 reduce-scatter.6
  281.4 57.8 reduce-scatter.4
  341.9 71.2 reduce-scatter.8
  415.8 72.2 reduce-scatter.10
  539.4 395.6 all-reduce.3
where the time goes:
time: 973 us; the launch traced here: 968 us
  waiting for transfers between devices  679 us (70%)
  matrix products  98.6 us (10%)
  local copies, waits for them, and re-layouts  81.8 us (8%)
  other arithmetic  67.5 us (7%)
  loops' own time  19.1 us (2%)
  between operations  14.6 us (2%)
    psum x1, waiting for transfers between devices, body(): total = lax.psum(flat, 'rep')  381 us
    reduce_scatter x1, waiting for transfers between devices, body(): lax.psum_scatter(joined.astype(jnp.bfloat16), 'shard', scatter_dimension=...  71.3 us
    reduce_scatter x1, waiting for transfers between devices, body(): lax.psum_scatter(grad_up.astype(jnp.bfloat16), 'shard', scatter_dimension...  69.8 us
    all_gather x1, waiting for transfers between devices, body(): full_up = lax.all_gather(w_up, 'shard', axis=1, tiled=True)  50.8 us
    all_gather x1, waiting for transfers between devices, body(): full_down = lax.all_gather(w_down, 'shard', axis=0, tiled=True)  48.4 us
    concatenate x1, other arithmetic, body(): flat = jnp.concatenate([o.reshape(-1).astype(jnp.float32) for o in owned])  48.4 us
    all_gather x1, waiting for transfers between devices, body(): full_qkv = lax.all_gather(w_qkv, 'shard', axis=1, tiled=True)  38.4 us
  transfers between devices with their start and end apart: 9, of which 7 were waited for; matrix products, arithmetic and copies ran while one was open for 15% of the time, Pallas kernels for 0%

commit v1 on v0

--- a/solution.py
+++ b/solution.py
@@ -256,7 +256,10 @@
     )
     owned = [qkv_own, out_own, up_own, joined_own]
     flat = jnp.concatenate([o.reshape(-1).astype(jnp.float32) for o in owned])
-    total = lax.psum(flat, "rep")
+    count, total = (lax.axis_size("rep"), flat)
+    for stride in [1 << k for k in range(count.bit_length() - 1)]:
+        pairs = [(i, i ^ stride) for i in range(count)]
+        total = total + lax.ppermute(total, "rep", pairs)
     pieces, offset = ([], 0)
     for o in owned:
         pieces.append(total[offset : offset + o.size].reshape(o.shape))

time: 973 us -> 1730 us (1.78)
  waiting for transfers between devices: 679 us -> 1380 us
  other arithmetic: 67.5 us -> 122 us
    ppermute x0 -> x3, waiting for transfers between devices: none -> 1070 us  [body(): total = total + lax.ppermute(total, 'rep', pairs)]
    psum x1 -> x0, waiting for transfers between devices: 381 us -> none  [body(): total = lax.psum(flat, 'rep')]
    add x0 -> x3, other arithmetic: none -> 60.2 us  [body(): total = total + lax.ppermute(total, 'rep', pairs)]
  transfers between devices with their start and end apart: 9 -> 11, of which waited for: 7 -> 9; matrix products, arithmetic and copies ran while one was open for 15% -> 8% of each run, Pallas kernels for 0% -> 0%
where the time goes in v1:
time: 1730 us; the launch traced here: 1720 us
  waiting for transfers between devices  1380 us (80%)
  other arithmetic  122 us (7%)
  matrix products  97.6 us (6%)
  local copies, waits for them, and re-layouts  81.3 us (5%)
  loops' own time  19 us (1%)
    ppermute x3, waiting for transfers between devices, body(): total = total + lax.ppermute(total, 'rep', pairs)  1070 us
    reduce_scatter x1, waiting for transfers between devices, body(): lax.psum_scatter(joined.astype(jnp.bfloat16), 'shard', scatter_dimension=...  72.7 us
    reduce_scatter x1, waiting for transfers between devices, body(): lax.psum_scatter(grad_up.astype(jnp.bfloat16), 'shard', scatter_dimension...  69.8 us
    add x3, other arithmetic, body(): total = total + lax.ppermute(total, 'rep', pairs)  60.2 us
    all_gather x1, waiting for transfers between devices, body(): full_up = lax.all_gather(w_up, 'shard', axis=1, tiled=True)  50.5 us
    all_gather x1, waiting for transfers between devices, body(): full_down = lax.all_gather(w_down, 'shard', axis=0, tiled=True)  48.5 us
    concatenate x1, other arithmetic, body(): flat = jnp.concatenate([o.reshape(-1).astype(jnp.float32) for o in owned])  46.8 us
    all_gather x1, waiting for transfers between devices, body(): full_qkv = lax.all_gather(w_qkv, 'shard', axis=1, tiled=True)  38.4 us
  transfers between devices with their start and end apart: 11, of which 9 were waited for; matrix products, arithmetic and copies ran while one was open for 8% of the time, Pallas kernels for 0%

profile of v1, /device:TPU:0, one launch (start us, length us, event | category | flops | bytes accessed | tf_op | source)
XLA Modules:
  0.0 1722.4 jit_solution(8200585163310472348)
XLA Ops:
  12.2 6.3 all-gather
  20.3 38.4 %all-gather.6.cloned.1.call-done = bf16[1024,3072]{1,0:T(8,128)(2,1)} async-done(((bf16[1024,768]{1,0:T(8,128)(2,1)}), bf16[1024,3072]{1,0:T(8,128)(2,1)}) %all-gather.6.cloned.1.call-update) | async-done | bytes 6291472 | tf_op jit(solution)/shard_map/all_gather | solution.py:165
  58.7 5.2 fusion.69
  66.0 1.5 copy.75
  68.5 19.0 %while.32 = (s32[]{:T(128)}, bf16[4,384,256]{1,2,0:T(8,128)(2,1)}, f32[4,4,384]{2,1,0:T(4,128)S(1)}, s32[4]{0:T(128)S(1)}, bf16[384,1024]{0,1:T(8,128)(2,1)S(1)}...) while((s32[]{:T(128)}, bf16[4,384,256]{1,2,0:T(8,128)(2,1)}, ...), condition=%wide.region_6.7_spmd.clone, body=%wide.region_3.6_spmd.clone.sunk | while | flops 157776416 | bytes 10964623 | solution.py:72
  88.8 3.1 fusion.80
  92.2 50.5 %all-gather.10.cloned.1.call-done = bf16[1024,4096]{1,0:T(8,128)(2,1)} async-done(((bf16[1024,1024]{1,0:T(8,128)(2,1)}), bf16[1024,4096]{1,0:T(8,128)(2,1)}) %all-gather.10.cloned.1.call-update) | async-done | bytes 8388624 | tf_op jit(solution)/shard_map/all_gather | solution.py:167
  142.7 11.3 fusion.30
  153.9 48.5 %all-gather.12.cloned.1.call-done = bf16[4096,1024]{1,0:T(8,128)(2,1)} async-done(((bf16[1024,1024]{1,0:T(8,128)(2,1)}), bf16[4096,1024]{1,0:T(8,128)(2,1)}) %all-gather.12.cloned.1.call-update) | async-done | bytes 8388624 | tf_op jit(solution)/shard_map/all_gather | solution.py:168
  202.4 10.9 fusion.81
  213.3 3.8 multiply_reduce_fusion.1
  219.4 2.6 convolution_convert_fusion.3
  222.1 2.6 convolution_convert_fusion.4
  227.5 49.4 %while.33 = (s32[]{:T(128)}, bf16[4,384,256]{1,2,0:T(8,128)(2,1)}, bf16[4,384,256]{1,2,0:T(8,128)(2,1)}, bf16[4,384,256]{1,2,0:T(8,128)(2,1)}, s32[4]{0:T(128)S(...) while((s32[]{:T(128)}, bf16[4,384,256]{1,2,0:T(8,128)(2,1)}, ...), condition=%wide.region_13.14_spmd.clone, body=%wide.region_11.13_spmd.clone.sunk | while | flops 385251872 | bytes 36898628 | solution.py:111
  235.6 1.1 multiply_reduce_fusion.5
  247.9 1.1 multiply_reduce_fusion.5
  272.5 1.1 multiply_reduce_fusion.5
  276.9 8.2 convolution_convert_fusion.2
  285.2 1.3 copy-done.5
  286.6 9.7 convolution_convert_fusion
  298.3 5.9 fusion.73
  304.3 1.2 copy-done.16
  306.8 4.7 copy.86
  311.5 6.6 convolution_convert_fusion.1
  318.2 3.8 fusion.15
  323.2 20.1 %reduce-scatter.5.cloned.1.call-done = bf16[1024,768]{1,0:T(8,128)(2,1)} async-done(((bf16[1024,3072]{1,0:T(8,128)(2,1)}), bf16[1024,768]{1,0:T(8,128)(2,1)}) %reduce-scatter.5.cloned.1.call-update) | async-done | bytes 1572880 | tf_op jit(solution)/shard_map/reduce_scatter | solution.py:248
  343.2 4.0 convert_element_type.308
  347.2 69.8 %reduce-scatter.9.cloned.1.call-done = bf16[1024,1024]{1,0:T(8,128)(2,1)} async-done(((bf16[1024,4096]{1,0:T(8,128)(2,1)}), bf16[1024,1024]{1,0:T(8,128)(2,1)}) %reduce-scatter.9.cloned.1.call-update) | async-done | bytes 2097168 | tf_op jit(solution)/shard_map/reduce_scatter | solution.py:254
  417.1 2.2 copy.98
  419.3 72.7 %reduce-scatter.11.cloned.1.call-done = bf16[1040,1024]{1,0:T(8,128)(2,1)} async-done(((bf16[4160,1024]{1,0:T(8,128)(2,1)}), bf16[1040,1024]{1,0:T(8,128)(2,1)}) %reduce-scatter.11.cloned.1.call-update) | async-done | bytes 2129936 | tf_op jit(solution)/shard_map/reduce_scatter | solution.py:245
  492.0 2.3 copy.99
  494.3 46.8 %maximum_convert_fusion = f32[3162112]{0:T(1024)S(1)} fusion(bf16[1064960]{0:T(1024)(128)(2,1)S(1)} %bitcast.226, bf16[1048576]{0:T(1024)(128)(2,1)S(1)} %bitcast.228, bf16[262144]{0:T(1024)(128)(2,1)S(1)} %bitcast.234, bf16[786432]{0:T(1024)(128)(2,1)S(1)} %copy-done.3), kind=kLoop, calls=%fused_computation.45 | loop fusion | flops 25296896 | bytes 18972672 | tf_op jit(solution)/shard_map/concatenate | solution.py:258
  541.1 1.5 collective-permute-start
  542.7 271.9 %collective-permute-done = f32[3162112]{0:T(1024)} collective-permute-done((f32[3162112]{0:T(1024)S(1)}, f32[3162112]{0:T(1024)}, u32[]{:S(2)}, u32[]{:S(2)}) %collective-permute-start) | collective-permute-done | bytes 12648480 | tf_op jit(solution)/shard_map/ppermute | solution.py:262
  814.6 48.6 %fusion.72 = f32[3162112]{0:T(1024)S(1)} fusion(f32[3162112]{0:T(1024)} %collective-permute-done, bf16[1064960]{0:T(1024)(128)(2,1)S(1)} %bitcast.227, bf16[1048576]{0:T(1024)(128)(2,1)S(1)} %bitcast.229, bf16[262144]{0:T(1024)(128)(2,1)S(1)} %bitcast.235, bf16[786432]{0:T(1024)(128)(2,1)S(1)} %copy-done.3), kind=kLoop, calls=%fused_computation.151 | loop fusion | flops 28459008 | bytes 31621120 | tf_op jit(solution)/shard_map/add | solution.py:262
  863.3 1.6 collective-permute-start.1
  864.9 271.1 %collective-permute-done.1 = f32[3162112]{0:T(1024)} collective-permute-done((f32[3162112]{0:T(1024)S(1)}, f32[3162112]{0:T(1024)}, u32[]{:S(2)}, u32[]{:S(2)}) %collective-permute-start.1) | collective-permute-done | bytes 12648480 | tf_op jit(solution)/shard_map/ppermute | solution.py:262
  1135.9 5.8 add.282
  1141.7 2.5 collective-permute-start.2
  1144.3 1.6 fusion.54
  1145.9 10.1 fusion.51
  1155.9 529.5 %collective-permute-done.2 = f32[3162112]{0:T(1024)} collective-permute-done((f32[3162112]{0:T(1024)S(1)}, f32[3162112]{0:T(1024)}, u32[]{:S(2)}, u32[]{:S(2)}) %collective-permute-start.2) | collective-permute-done | bytes 12648480 | tf_op jit(solution)/shard_map/ppermute | solution.py:262
  1685.4 5.8 add.283
  1691.9 2.2 slice.159
  1694.1 4.4 fusion.79
  1699.8 4.7 reshape.407
  1705.6 4.9 slice.140
  1710.5 4.9 slice.143
  (311 shorter events, 70.1 us)
Async XLA Ops:
  7.2 51.5 %all-gather.6.cloned.1.call-start = ((), (), s32[]{:S(2)}) async-start(), calls=%async_computation.4 | async-start | bytes 7864320 | tf_op jit(solution)/shard_map/all_gather | solution.py:165
  7.9 2.3 copy-start.26
  7.9 2.5 copy-start.27
  7.9 2.7 copy-start.28
  7.9 2.9 copy-start.29
  8.0 3.1 copy-start.30
  8.0 3.4 copy-start.31
  8.0 3.6 copy-start.32
  8.0 3.8 copy-start.25
  8.0 4.0 copy-start.33
  8.0 79.6 %all-gather.8.cloned.1.call-start = ((), (), s32[]{:S(2)}) async-start(), calls=%async_computation.5 | async-start | bytes 2621440 | tf_op jit(solution)/shard_map/all_gather | solution.py:166
  8.8 10.5 copy-start.24
  8.8 10.9 copy-start.1
  8.8 133.9 %all-gather.10.cloned.1.call-start = ((), (), s32[]{:S(2)}) async-start(), calls=%async_computation.6 | async-start | bytes 10485760 | tf_op jit(solution)/shard_map/all_gather | solution.py:167
  9.5 192.9 %all-gather.12.cloned.1.call-start = ((), (), s32[]{:S(2)}) async-start(), calls=%async_computation.7 | async-start | bytes 10485760 | tf_op jit(solution)/shard_map/all_gather | solution.py:168
  10.1 311.9 %reduce-scatter.7.cloned.1.call-start = ((), (), s32[]{:S(2)}) async-start(), calls=%async_computation.9 | async-start | bytes 2621440 | tf_op jit(solution)/shard_map/reduce_scatter | solution.py:251
  91.9 125.3 %copy-start.4 = (f32[384,1024]{1,0:T(8,128)}, f32[384,1024]{1,0:T(8,128)S(1)}, u32[]{:S(2)}) copy-start(f32[384,1024]{1,0:T(8,128)S(1)} %get-tuple-element.523) | copy-start | bytes 4718596
  142.7 59.7 %copy-start.13 = (bf16[1,384,1024]{2,1,0:T(8,128)(2,1)S(1)}, bf16[1,384,1024]{2,1,0:T(8,128)(2,1)}, u32[]{:S(2)}) copy-start(bf16[1,384,1024]{2,1,0:T(8,128)(2,1)} %param.22) | copy-start | bytes 2359300
  202.4 10.9 copy-start.34
  213.3 3.8 copy-start.35
  217.7 1.7 copy-start.20
  222.0 121.2 %reduce-scatter.5.cloned.1.call-start = ((), (), s32[]{:S(2)}) async-start(), calls=%async_computation.8 | async-start | bytes 7864320 | tf_op jit(solution)/shard_map/reduce_scatter | solution.py:248
  227.7 3.5 copy-start.21
  238.2 1.9 copy-start.12
  238.2 1.9 copy-start.22
  240.0 3.5 copy-start.21
  250.5 1.9 copy-start.12
  250.5 1.9 copy-start.22
  252.3 3.5 copy-start.21
  262.7 1.9 copy-start.12
  262.7 1.9 copy-start.22
  264.6 3.5 copy-start.21
  275.0 1.9 copy-start.12
  275.0 1.9 copy-start.22
  285.2 131.9 %reduce-scatter.9.cloned.1.call-start = ((), (), s32[]{:S(2)}) async-start(), calls=%async_computation.10 | async-start | bytes 10485760 | tf_op jit(solution)/shard_map/reduce_scatter | solution.py:254
  296.2 1.8 copy-start.18
  296.2 2.1 copy-start.19
  296.2 195.8 %reduce-scatter.11.cloned.1.call-start = ((), (), s32[]{:S(2)}) async-start(), calls=%async_computation.11 | async-start | bytes 10649600 | tf_op jit(solution)/shard_map/reduce_scatter | solution.py:245
  492.0 2.3 copy-start.3
  541.1 273.5 %collective-permute-start = (f32[3162112]{0:T(1024)S(1)}, f32[3162112]{0:T(1024)}, u32[]{:S(2)}, u32[]{:S(2)}) collective-permute-start(f32[3162112]{0:T(1024)S(1)} %maximum_convert_fusion), channel_id=1, source_target_pairs={{0,4},{4,0},{8,12},{12,8},{16,20},{20,16},{24,28},{28,24},{1,5},{5... | collective-permute-start | bytes 37945352 | tf_op jit(solution)/shard_map/ppermute | solution.py:262
  863.2 281.0 %copy-start.23 = (f32[1,2,4,128]{3,2,1,0:T(4,128)S(1)}, f32[1,2,4,128]{3,2,1,0:T(4,128)}, u32[]{:S(2)}) copy-start(f32[1,2,4,128]{3,2,1,0:T(4,128)} %get-tuple-element.514) | copy-start | bytes 12292
  863.3 281.0 %copy-start.8 = (f32[384,1024]{1,0:T(8,128)S(1)}, f32[384,1024]{1,0:T(8,128)}, u32[]{:S(2)}) copy-start(f32[384,1024]{1,0:T(8,128)} %copy-done.7) | copy-start | bytes 4718596
  863.3 281.0 %copy-start.15 = (bf16[1,384,1024]{2,1,0:T(8,128)(2,1)S(1)}, bf16[1,384,1024]{2,1,0:T(8,128)(2,1)}, u32[]{:S(2)}) copy-start(bf16[1,384,1024]{2,1,0:T(8,128)(2,1)} %param.22) | copy-start | bytes 2359300
  863.3 281.0 %copy-start.17 = (f32[384,1024]{1,0:T(8,128)S(1)}, f32[384,1024]{1,0:T(8,128)}, u32[]{:S(2)}) copy-start(f32[384,1024]{1,0:T(8,128)} %copy-done.16) | copy-start | bytes 4718596
  863.3 272.6 %collective-permute-start.1 = (f32[3162112]{0:T(1024)S(1)}, f32[3162112]{0:T(1024)}, u32[]{:S(2)}, u32[]{:S(2)}) collective-permute-start(f32[3162112]{0:T(1024)S(1)} %fusion.72), channel_id=1, source_target_pairs={{0,8},{4,12},{8,0},{12,4},{16,24},{20,28},{24,16},{28,20},{1,9},{5... | collective-permute-start | bytes 37945352 | tf_op jit(solution)/shard_map/ppermute | solution.py:262
  1141.7 543.7 %collective-permute-start.2 = (f32[3162112]{0:T(1024)S(1)}, f32[3162112]{0:T(1024)}, u32[]{:S(2)}, u32[]{:S(2)}) collective-permute-start(f32[3162112]{0:T(1024)S(1)} %add.282), channel_id=1, source_target_pairs={{0,16},{4,20},{8,24},{12,28},{16,0},{20,4},{24,8},{28,12},{1,17},{... | collective-permute-start | bytes 37945352 | tf_op jit(solution)/shard_map/ppermute | solution.py:262
  1691.2 8.0 copy-start
  1699.8 4.7 slice-start
  (12 other events, 15.6 us)
Sparse Core Ops, SparseCore 0:
  9.6 49.0 all-gather.5
  60.2 22.5 all-gather.7
  84.4 58.2 all-gather.9
  144.1 58.2 all-gather.11
  222.1 31.2 reduce-scatter.6
  285.3 57.9 reduce-scatter.4
  345.8 71.2 reduce-scatter.8
  419.7 72.2 reduce-scatter.10
